TPU v7x, 32 devices: a whole 2x2x4 slice. The times are simulated.
32 devices in a mesh: pb: 8 (over z, y), col: 4 (over x, core).
Axes of the slice: x: 2, y: 2, z: 4, core: 2. Of those that a mesh axis runs over, the one named last changes fastest.
Arguments:
- orbitals: bfloat16 [8, 48, 4096], P('pb', None, 'col'), may hold values from -6 to 6
- screening: bfloat16 [8, 4096, 4096], P('pb', None, 'col'), may hold values from -0.0014648438 to 0.0014648438
- pairs_k: int32 [8, 4], P('pb'), may hold values from 0 to 7
Outputs:
- kernel: float32 [8, 4, 256, 1024], P('pb', None, None, 'col')
All inputs are finite; a program needn't handle non-finite values.
Results may differ from a plain program's by a relative error of at most 0.0049.
Values may be sent and summed in bfloat16 or wider, within the bound.
No kernel may reach another device: no remote copies, remote signals or barrier semaphores. Data moves between devices by JAX's collectives and lax.ppermute only.
A program may use at most 128 MiB of HBM per device.

v0:
```python
import jax
import jax.numpy as jnp
from jax import lax
from jax.sharding import PartitionSpec as P

NV = 16
NC = 32


def body(orbitals, screening, pairs_k):
    k_dev, orb_count, mu_cols = orbitals.shape
    group_count = lax.axis_size("pb")
    kpoint_count = k_dev * group_count
    group_index = lax.axis_index("pb")
    kpoint_a = pairs_k[0]
    kpoint_b = (kpoint_a - group_index) % kpoint_count
    wanted = jnp.concatenate([kpoint_a, kpoint_b])
    slot_count = wanted.shape[0]
    pair_count = slot_count // 2
    block_rows = lax.all_gather(orbitals, "pb", axis=0, tiled=True)
    indices = jnp.arange(block_rows.shape[0], dtype=jnp.int32)
    chooser = (wanted[:, None] == indices[None, :]).astype(jnp.bfloat16)
    fetched = jnp.einsum(
        "sk,kom->som", chooser, block_rows, preferred_element_type=jnp.float32
    ).astype(jnp.bfloat16)
    valence = lax.all_gather(fetched[:, :NV, :], "col", axis=2, tiled=True)
    valence_a = valence[:pair_count].astype(jnp.float32)
    valence_b = valence[pair_count:].astype(jnp.float32)
    val_pairs = (valence_a[:, :, None, :] * valence_b[:, None, :, :]).astype(jnp.bfloat16)
    val_pairs = val_pairs.reshape(pair_count * NV * NV, valence.shape[2])
    screened = jnp.dot(val_pairs, screening[0], preferred_element_type=jnp.float32).astype(
        jnp.bfloat16
    )
    screened = screened.reshape(pair_count, NV * NV, mu_cols)
    conduction = fetched[:, NV:, :].astype(jnp.float32)
    cond_pairs = (conduction[:pair_count, :, None, :] * conduction[pair_count:, None, :, :]).astype(
        jnp.bfloat16
    )
    cond_pairs = cond_pairs.reshape(pair_count, NC * NC, mu_cols)
    partial_value = jnp.einsum(
        "pan,pbn->pab", screened, cond_pairs, preferred_element_type=jnp.float32
    )
    whole_sum = lax.psum(partial_value, "col")
    column_count = whole_sum.shape[2] // lax.axis_size("col")
    result = lax.dynamic_slice_in_dim(
        whole_sum, lax.axis_index("col") * column_count, column_count, 2
    )
    return result[None]


def solution(mesh):
    placed = (P("pb", None, "col"), P("pb", None, "col"), P("pb", None))
    return jax.shard_map(
        body, mesh=mesh, in_specs=placed, out_specs=P("pb", None, None, "col"), check_vma=False
    )
```

profile of v0, /device:TPU:0, one launch (start us, length us, event | category | flops | bytes accessed | tf_op | source)
XLA Modules:
  0.0 181.1 jit_solution(12685223790277849974)
XLA Ops:
  6.5 0.0 all-gather.2.cloned.1.call-start
  6.5 34.0 %all_gather.6 = bf16[8,48,1024]{2,1,0:T(8,128)(2,1)S(1)} all-gather(bf16[1,48,1024]{2,1,0:T(8,128)(2,1)} %param.3), channel_id=1, replica_groups=mesh['pb'=8,'col'=4] {'pb'}, dimensions={0}, use_global_device_ids=true | all-gather | bytes 884736 | tf_op jit(solution)/shard_map/all_gather | solution.py:20
  40.5 0.7 and_select_fusion
  41.2 0.7 pad_add_fusion
  41.9 0.6 fusion.5
  42.5 0.4 copy.19
  42.9 0.7 slice.24
  43.6 0.0 all-gather.2.cloned.1.call-update
  43.7 0.0 all-reduce.2.cloned.1.call-start
  43.7 0.1 slice_convert_fusion
  43.8 0.1 fusion.11
  43.9 6.2 %multiply_convert_fusion = bf16[4,32,32,1024]{3,2,1,0:T(8,128)(2,1)} fusion(f32[4,32,1024]{2,1,0:T(8,128)S(1)} %get-tuple-element.6, f32[4,32,1024]{2,1,0:T(8,128)S(1)} %get-tuple-element.5), kind=kLoop, calls=%fused_computation | loop fusion | flops 8388608 | bytes 9437184 | tf_op jit(solution)/shard_map/convert_element_type | solution.py:36
  50.2 11.4 %all-gather.2.cloned.1.call-done = bf16[8,16,4096]{2,1,0:T(8,128)(2,1)} async-done(((bf16[8,16,1024]{2,1,0:T(8,128)(2,1)}), bf16[8,16,4096]{2,1,0:T(8,128)(2,1)}) %all-gather.2.cloned.1.call-update) | async-done | bytes 1048592 | tf_op jit(solution)/shard_map/all_gather | solution.py:26
  61.6 1.4 slice_convert_fusion.2
  63.0 0.0 slice-start
  63.0 5.2 %multiply_convert_fusion.1 = bf16[4,16,16,4096]{3,2,1,0:T(8,128)(2,1)} fusion(f32[4,16,4096]{2,1,0:T(8,128)S(1)} %get-tuple-element.8, f32[4,16,4096]{2,1,0:T(8,128)S(1)} %get-tuple-element.7), kind=kLoop, calls=%fused_computation.1 | loop fusion | flops 8388608 | bytes 10485760 | tf_op jit(solution)/shard_map/convert_element_type | solution.py:29
  68.2 0.0 slice-start.1
  68.2 13.8 %fusion.2 = bf16[1024,1024]{1,0:T(8,128)(2,1)S(1)} fusion(bf16[1024,4096]{1,0:T(8,128)(2,1)} %bitcast.21, bf16[1,4096,1024]{2,1,0:T(8,128)(2,1)} %param.4), kind=kOutput, calls=%fused_computation.4 | convolution fusion | flops 8590983168 | bytes 18874368 | tf_op jit(solution)/shard_map/dot_general | solution.py:31
  82.0 0.0 slice-done
  82.0 0.0 slice-done.1
  82.0 4.4 %fusion.12 = f32[4,256,1024]{2,1,0:T(8,128)} fusion(bf16[4,256,1024]{2,1,0:T(8,128)(2,1)S(1)} %bitcast.22, bf16[4,1024,1024]{2,1,0:T(8,128)(2,1)S(1)} %bitcast.20), kind=kOutput, calls=%fused_computation.21 | convolution fusion | flops 2147483648 | bytes 14680064 | tf_op jit(solution)/shard_map/pan,pbn->pab/dot_general | solution.py:40
  86.4 0.0 all-reduce.2.cloned.1.call-update
  86.4 85.6 %all-reduce.2.cloned.1.call-done = f32[4,256,1024]{2,1,0:T(8,128)} async-done(((f32[4,256,1024]{2,1,0:T(8,128)}), f32[4,256,1024]{2,1,0:T(8,128)}) %all-reduce.2.cloned.1.call-update) | async-done | bytes 4194320 | tf_op jit(solution)/shard_map/psum | solution.py:43
  172.0 2.3 %dynamic-slice_bitcast_fusion = f32[1,4,256,256]{3,2,1,0:T(8,128)} fusion(f32[4,256,1024]{2,1,0:T(8,128)} %all-reduce.2.cloned.1.call-done, s32[]{:T(128)S(6)} %select_n.11), kind=kLoop, calls=%fused_computation.6 | loop fusion | bytes 2097156 | tf_op jit(solution)/shard_map/broadcast_in_dim | solution.py:48
  (1 shorter events, 0.0 us)
Async XLA Ops:
  6.5 55.0 %all-gather.2.cloned.1.call-start = ((), (), s32[]{:S(2)}) async-start(), calls=%async_computation | async-start | bytes 1310720 | tf_op jit(solution)/shard_map/all_gather | solution.py:26
  43.7 128.3 %all-reduce.2.cloned.1.call-start = ((), (), s32[]{:S(2)}) async-start(), calls=%async_computation.1 | async-start | bytes 8388608 | tf_op jit(solution)/shard_map/psum | solution.py:43
  63.0 19.0 %slice-start = ((s8[8388608]{0:T(1024)(128)(4,1)}), s8[4194304]{0:T(1024)(128)(4,1)S(1)}, s32[]{:S(2)}) async-start(s8[8388608]{0:T(1024)(128)(4,1)} %bitcast.18), calls=%async_computation.2 | async-start | bytes 8388608
  68.2 13.8 %slice-start.1 = ((s8[8388608]{0:T(1024)(128)(4,1)}), s8[4194304]{0:T(1024)(128)(4,1)S(1)}, s32[]{:S(2)}) async-start(s8[8388608]{0:T(1024)(128)(4,1)} %bitcast.18), calls=%async_computation.3 | async-start | bytes 8388608
Sparse Core Ops, SparseCore 0:
  43.8 17.7 all-gather.1
  86.5 85.4 all-reduce.1
where the time goes:
time: 181 us
  waiting for transfers between devices  97 us (54%)
  blocking collectives  34 us (19%)
  matrix products  18.7 us (10%)
  other arithmetic  14.3 us (8%)
  between operations  13.5 us (7%)
  local copies, waits for them, and re-layouts  3.56 us (2%)
    psum x1, waiting for transfers between devices, body(): whole_sum = lax.psum(partial_value, 'col')  85.6 us
    all_gather x1, blocking collectives, body(): block_rows = lax.all_gather(orbitals, 'pb', axis=0, tiled=True)  34 us
    dot_general x1, matrix products, body(): jnp.dot(val_pairs, screening[0], preferred_element_type=jnp.float32)  13.8 us
    all_gather x1, waiting for transfers between devices, body(): valence = lax.all_gather(fetched[:, :NV, :], 'col', axis=2, tiled=True)  11.4 us
    convert_element_type x1, other arithmetic, body(): (conduction[:pair_count, :, None, :] * conduction[pair_count:, None, :, :...  6.24 us
    convert_element_type x1, other arithmetic, body(): (valence_a[:, :, None, :] * valence_b[:, None, :, :]).astype(jnp.bfloat16)  5.17 us
    dot_general x1, matrix products, body(): jnp.einsum('pan,pbn->pab', screened, cond_pairs, preferred_element_type=j...  4.36 us
  transfers between devices with their start and end apart: 2, of which 2 were waited for; matrix products, arithmetic and copies ran while one was open for 4% of the time, Pallas kernels for 0%

commit v1 on v0

--- a/solution.py
+++ b/solution.py
@@ -40,7 +40,8 @@
     partial_value = jnp.einsum(
         "pan,pbn->pab", screened, cond_pairs, preferred_element_type=jnp.float32
     )
-    whole_sum = lax.psum(partial_value, "col")
+    parts = lax.all_gather(partial_value, "col")
+    whole_sum = jnp.sum(parts, axis=0)
     column_count = whole_sum.shape[2] // lax.axis_size("col")
     result = lax.dynamic_slice_in_dim(
         whole_sum, lax.axis_index("col") * column_count, column_count, 2

time: 181 us -> 212 us (1.17)
  waiting for transfers between devices: 97 us -> 118 us
  other arithmetic: 14.3 us -> 24.6 us
    all_gather x0 -> x1, waiting for transfers between devices: none -> 106 us  [body(): parts = lax.all_gather(partial_value, 'col')]
    psum x1 -> x0, waiting for transfers between devices: 85.6 us -> none  [body(): whole_sum = lax.psum(partial_value, 'col')]
    reduce_sum x0 -> x1, other arithmetic: none -> 10.3 us  [body(): whole_sum = jnp.sum(parts, axis=0)]
  transfers between devices with their start and end apart: 2 -> 2, of which waited for: 2 -> 2; matrix products, arithmetic and copies ran while one was open for 4% -> 3% of each run, Pallas kernels for 0% -> 0%
where the time goes in v1:
time: 212 us
  waiting for transfers between devices  118 us (56%)
  blocking collectives  34 us (16%)
  other arithmetic  24.6 us (12%)
  matrix products  18.7 us (9%)
  between operations  13.5 us (6%)
  local copies, waits for them, and re-layouts  3.56 us (2%)
    all_gather x1, waiting for transfers between devices, body(): parts = lax.all_gather(partial_value, 'col')  106 us
    all_gather x1, blocking collectives, body(): block_rows = lax.all_gather(orbitals, 'pb', axis=0, tiled=True)  34 us
    dot_general x1, matrix products, body(): jnp.dot(val_pairs, screening[0], preferred_element_type=jnp.float32)  13.8 us
    all_gather x1, waiting for transfers between devices, body(): valence = lax.all_gather(fetched[:, :NV, :], 'col', axis=2, tiled=True)  11.4 us
    reduce_sum x1, other arithmetic, body(): whole_sum = jnp.sum(parts, axis=0)  10.3 us
    convert_element_type x1, other arithmetic, body(): (conduction[:pair_count, :, None, :] * conduction[pair_count:, None, :, :...  6.24 us
    convert_element_type x1, other arithmetic, body(): (valence_a[:, :, None, :] * valence_b[:, None, :, :]).astype(jnp.bfloat16)  5.17 us
    dot_general x1, matrix products, body(): jnp.einsum('pan,pbn->pab', screened, cond_pairs, preferred_element_type=j...  4.33 us
  transfers between devices with their start and end apart: 2, of which 2 were waited for; matrix products, arithmetic and copies ran while one was open for 3% of the time, Pallas kernels for 0%

profile of v1, /device:TPU:0, one launch (start us, length us, event | category | flops | bytes accessed | tf_op | source)
XLA Modules:
  0.0 211.8 jit_solution(11526990211560439759)
XLA Ops:
  6.5 0.0 all-gather.4.cloned.1.call-start
  6.5 34.0 %all_gather.12 = bf16[8,48,1024]{2,1,0:T(8,128)(2,1)S(1)} all-gather(bf16[1,48,1024]{2,1,0:T(8,128)(2,1)} %param.3), channel_id=1, replica_groups=mesh['pb'=8,'col'=4] {'pb'}, dimensions={0}, use_global_device_ids=true | all-gather | bytes 884736 | tf_op jit(solution)/shard_map/all_gather | solution.py:20
  40.5 0.7 and_select_fusion
  41.2 0.7 pad_add_fusion
  41.9 0.6 fusion.5
  42.5 0.4 copy.19
  42.9 0.7 slice.24
  43.6 0.0 all-gather.4.cloned.1.call-update
  43.7 0.0 all-gather.6.cloned.1.call-start
  43.7 0.1 slice_convert_fusion
  43.8 0.1 fusion.11
  43.9 6.2 %multiply_convert_fusion = bf16[4,32,32,1024]{3,2,1,0:T(8,128)(2,1)} fusion(f32[4,32,1024]{2,1,0:T(8,128)S(1)} %get-tuple-element.6, f32[4,32,1024]{2,1,0:T(8,128)S(1)} %get-tuple-element.5), kind=kLoop, calls=%fused_computation | loop fusion | flops 8388608 | bytes 9437184 | tf_op jit(solution)/shard_map/convert_element_type | solution.py:36
  50.2 11.4 %all-gather.4.cloned.1.call-done = bf16[8,16,4096]{2,1,0:T(8,128)(2,1)} async-done(((bf16[8,16,1024]{2,1,0:T(8,128)(2,1)}), bf16[8,16,4096]{2,1,0:T(8,128)(2,1)}) %all-gather.4.cloned.1.call-update) | async-done | bytes 1048592 | tf_op jit(solution)/shard_map/all_gather | solution.py:26
  61.6 1.4 slice_convert_fusion.2
  63.0 0.0 slice-start
  63.0 5.2 %multiply_convert_fusion.1 = bf16[4,16,16,4096]{3,2,1,0:T(8,128)(2,1)} fusion(f32[4,16,4096]{2,1,0:T(8,128)S(1)} %get-tuple-element.8, f32[4,16,4096]{2,1,0:T(8,128)S(1)} %get-tuple-element.7), kind=kLoop, calls=%fused_computation.1 | loop fusion | flops 8388608 | bytes 10485760 | tf_op jit(solution)/shard_map/convert_element_type | solution.py:29
  68.2 0.0 slice-start.1
  68.2 13.8 %fusion.2 = bf16[1024,1024]{1,0:T(8,128)(2,1)S(1)} fusion(bf16[1024,4096]{1,0:T(8,128)(2,1)} %bitcast.23, bf16[1,4096,1024]{2,1,0:T(8,128)(2,1)} %param.4), kind=kOutput, calls=%fused_computation.4 | convolution fusion | flops 8590983168 | bytes 18874368 | tf_op jit(solution)/shard_map/dot_general | solution.py:31
  82.0 0.0 slice-done
  82.0 0.0 slice-done.1
  82.0 4.3 %fusion.12 = f32[4,256,1024]{2,1,0:T(8,128)} fusion(bf16[4,256,1024]{2,1,0:T(8,128)(2,1)S(1)} %bitcast.24, bf16[4,1024,1024]{2,1,0:T(8,128)(2,1)S(1)} %bitcast.21), kind=kOutput, calls=%fused_computation.21 | convolution fusion | flops 2147483648 | bytes 14680064 | tf_op jit(solution)/shard_map/pan,pbn->pab/dot_general | solution.py:40
  86.3 0.0 all-gather.6.cloned.1.call-update
  86.4 106.1 %all-gather.6.cloned.1.call-done = f32[16,256,1024]{2,1,0:T(8,128)} async-done(((f32[4,256,1024]{2,1,0:T(8,128)}), f32[16,256,1024]{2,1,0:T(8,128)}) %all-gather.6.cloned.1.call-update) | async-done | bytes 16777232 | tf_op jit(solution)/shard_map/all_gather | solution.py:43
  192.4 10.3 %reduce_sum.9 = f32[4,256,1024]{2,1,0:T(8,128)} reduce(f32[4,4,256,1024]{3,2,1,0:T(8,128)} %bitcast.22, f32[]{:T(128)} %constant.27.clone.1), dimensions={0}, to_apply=%region_0.1 | reduce | flops 3145728 | bytes 20971524 | tf_op jit(solution)/shard_map/reduce_sum | solution.py:44
  202.7 2.3 %dynamic-slice_bitcast_fusion = f32[1,4,256,256]{3,2,1,0:T(8,128)} fusion(f32[4,256,1024]{2,1,0:T(8,128)} %reduce_sum.9, s32[]{:T(128)S(6)} %select_n.11), kind=kLoop, calls=%fused_computation.6 | loop fusion | bytes 2097156 | tf_op jit(solution)/shard_map/broadcast_in_dim | solution.py:49
  (1 shorter events, 0.0 us)
Async XLA Ops:
  6.5 55.0 %all-gather.4.cloned.1.call-start = ((), (), s32[]{:S(2)}) async-start(), calls=%async_computation | async-start | bytes 1310720 | tf_op jit(solution)/shard_map/all_gather | solution.py:26
  43.7 148.8 %all-gather.6.cloned.1.call-start = ((), (), s32[]{:S(2)}) async-start(), calls=%async_computation.1 | async-start | bytes 20971520 | tf_op jit(solution)/shard_map/all_gather | solution.py:43
  63.0 19.0 %slice-start = ((s8[8388608]{0:T(1024)(128)(4,1)}), s8[4194304]{0:T(1024)(128)(4,1)S(1)}, s32[]{:S(2)}) async-start(s8[8388608]{0:T(1024)(128)(4,1)} %bitcast.19), calls=%async_computation.2 | async-start | bytes 8388608
  68.2 13.8 %slice-start.1 = ((s8[8388608]{0:T(1024)(128)(4,1)}), s8[4194304]{0:T(1024)(128)(4,1)S(1)}, s32[]{:S(2)}) async-start(s8[8388608]{0:T(1024)(128)(4,1)} %bitcast.19), calls=%async_computation.3 | async-start | bytes 8388608
Sparse Core Ops, SparseCore 0:
  43.8 17.7 all-gather.3
  86.5 105.9 all-gather.5
